TPU v7x, 128 devices: a whole 4x4x4 slice. The times are simulated.
128 devices in a mesh: row: 32 (over y, z_lo, x), col: 4 (over z_hi, core).
Axes of the slice: x: 4, y: 4, z: 4 (z_hi: 2, z_lo: 2; z = z_hi * 2 + z_lo), core: 2. Of those that a mesh axis runs over, the one named last changes fastest.
Arguments:
- ratings: bfloat16 [4, 262144, 512], P(None, ('row', 'col'))
- tile_mask: int32 [4, 2048, 4], P(None, ('row', 'col')), may hold values from 0 to 1, as said below
- tile_counts: int32 [128], replicated, may hold values from 1 to 16, as said below
- users: float32 [131072, 128], P(('row', 'col')), may hold values from -2 to 2
- user_accum: float32 [131072, 128], P(('row', 'col')), may hold values from 0.05 to 0.5
- items: float32 [65536, 128], P(('row', 'col')), may hold values from -2 to 2
- item_accum: float32 [65536, 128], P(('row', 'col')), may hold values from 0.05 to 0.5
Outputs:
- users_out: float32 [131072, 128], P(('row', 'col'))
- user_accum_out: float32 [131072, 128], P(('row', 'col'))
- items_out: float32 [65536, 128], P(('row', 'col'))
- item_accum_out: float32 [65536, 128], P(('row', 'col'))
- losses: float32 [4], replicated
Inputs may be any that keep to these rules, and one draw needn't show every extreme that they name: Each group of 4 positions has tile_counts summing to 32, and exactly one position of each group, not always the same, owns 2 * 8 tiles. `tile_mask`: in each stratum, the first slot's first item tile of every position is 1.
All inputs are finite; a program needn't handle non-finite values.
Results may differ from a plain program's by a relative error of at most 0.0025.
Values sent between devices are 32-bit elements; how exact they have to be, the bound alone decides.
No kernel may reach another device: no remote copies, remote signals or barrier semaphores. Data moves between devices by JAX's collectives and lax.ppermute only.
A program may use at most 64 MiB of HBM per device.

v0:
```python
import jax
import jax.numpy as jnp
from jax import lax
from jax.sharding import PartitionSpec as P

TILE = 128
UT = 8
STEPS = 3
ridge_weight = 0.02
step_rate = 0.05


def passed_along(value, axis, steps):
    count = lax.axis_size(axis)
    pairs = [(source, (source + steps) % count) for source in range(count)]
    return lax.ppermute(value, axis, pairs)


def update(user_fac, user_acc, item_fac, item_acc, rating_block, live_tiles):
    tile_size = user_fac.shape[0] // live_tiles.shape[0]
    user_half = user_fac.astype(jnp.bfloat16)
    item_half = item_fac.astype(jnp.bfloat16)
    predicted = lax.dot_general(
        user_half, item_half, (((1,), (1,)), ((), ())), preferred_element_type=jnp.float32
    )
    residue = predicted - rating_block.astype(jnp.float32)
    masked = (
        residue.reshape(live_tiles.shape[0], tile_size, live_tiles.shape[1], tile_size)
        * live_tiles[:, None, :, None]
    ).reshape(residue.shape)
    sq_error = jnp.sum(masked * residue)
    err_half = masked.astype(jnp.bfloat16)
    grad_user = (
        jnp.dot(err_half, item_half, preferred_element_type=jnp.float32)
        * float(item_fac.shape[0]) ** (-0.5)
        + ridge_weight * user_fac
    )
    grad_item = (
        lax.dot_general(
            err_half, user_half, (((0,), (0,)), ((), ())), preferred_element_type=jnp.float32
        )
        * float(UT * TILE) ** (-0.5)
        + ridge_weight * item_fac
    )
    user_acc = user_acc + grad_user * grad_user
    item_acc = item_acc + grad_item * grad_item
    user_fac = user_fac - step_rate * grad_user * lax.rsqrt(user_acc)
    item_fac = item_fac - step_rate * grad_item * lax.rsqrt(item_acc)
    return (user_fac, user_acc, item_fac, item_acc, sq_error)


def on_device(ratings, tile_mask, tile_counts, users, user_accum, items, item_accum):
    strata_count = ratings.shape[0]
    slot_count = tile_mask.shape[1]
    tile_size = ratings.shape[1] // slot_count
    group_size = lax.axis_size("col")
    member = lax.axis_index("col")
    arrived_rows = users.shape[0]
    group_counts = lax.dynamic_slice_in_dim(
        tile_counts, lax.axis_index("row") * group_size, group_size
    )
    ranks = jnp.arange(group_size, dtype=jnp.int32)
    start_tile = jnp.sum(jnp.where(ranks < member, group_counts, 0))
    own_count = jnp.sum(jnp.where(ranks == member, group_counts, 0))
    valid = (jnp.arange(slot_count, dtype=jnp.int32) < own_count).astype(jnp.float32)
    whole_pair = lax.all_gather(jnp.stack([users, user_accum]), "col", axis=1, tiled=True)
    pad_rows = slot_count * tile_size
    ext_pair = jnp.concatenate([whole_pair, whole_pair[:, :pad_rows]], axis=1)
    user_pair = lax.dynamic_slice_in_dim(ext_pair, start_tile * tile_size, pad_rows, 1)
    user_fac = user_pair[0]
    user_acc = user_pair[1]
    held_pair = jnp.stack([items, item_accum])
    loss_list = []
    for stratum in range(strata_count):
        live_tiles = tile_mask[stratum].astype(jnp.float32) * valid[:, None]
        item_fac = held_pair[0]
        item_acc = held_pair[1]
        for inner in range(STEPS):
            user_fac, user_acc, item_fac, item_acc, sq_error = update(
                user_fac, user_acc, item_fac, item_acc, ratings[stratum], live_tiles
            )
            if inner == 0:
                observed = jnp.sum(live_tiles) * float(tile_size * tile_size)
                loss_list.append(jnp.stack([sq_error, observed]))
        held_pair = jnp.stack([item_fac, item_acc])
        if stratum + 1 < strata_count:
            held_pair = passed_along(held_pair, ("row", "col"), 1)
    loss_parts = lax.psum(jnp.stack(loss_list), ("row", "col"))
    losses = loss_parts[:, 0] / loss_parts[:, 1]
    row_valid = jnp.repeat(valid, tile_size)[None, :, None] > 0.5
    kept_pair = jnp.where(row_valid, jnp.stack([user_fac, user_acc]), 0.0)
    frame_rows = group_size * arrived_rows + pad_rows
    frame_pair = lax.dynamic_update_slice_in_dim(
        jnp.zeros((2, frame_rows, kept_pair.shape[2]), jnp.float32),
        kept_pair,
        start_tile * tile_size,
        1,
    )
    users_pair = lax.psum_scatter(
        frame_pair[:, : group_size * arrived_rows], "col", scatter_dimension=1, tiled=True
    )
    return (users_pair[0], users_pair[1], held_pair[0], held_pair[1], losses)


def solution(mesh):
    return jax.shard_map(
        on_device,
        mesh=mesh,
        in_specs=(
            P(None, ("row", "col"), None),
            P(None, ("row", "col"), None),
            P(),
            P(("row", "col"), None),
            P(("row", "col"), None),
            P(("row", "col"), None),
            P(("row", "col"), None),
        ),
        out_specs=(
            P(("row", "col"), None),
            P(("row", "col"), None),
            P(("row", "col"), None),
            P(("row", "col"), None),
            P(),
        ),
        check_vma=False,
    )
```

profile of v0, /device:TPU:1, one launch (start us, length us, event | category | flops | bytes accessed | tf_op | source)
XLA Modules:
  0.0 256.5 jit_solution(1015268047695154100)
XLA Ops:
  7.2 2.3 pad_maximum_fusion
  9.6 0.7 fusion.116
  11.0 0.7 compare_convert_fusion
  11.6 0.7 fusion.121
  12.4 39.6 %all-gather.2.cloned.1.call-done = f32[2,4096,128]{2,1,0:T(8,128)} async-done(((f32[2,1024,128]{2,1,0:T(8,128)}), f32[2,4096,128]{2,1,0:T(8,128)}) %all-gather.2.cloned.1.call-update) | async-done | bytes 4194320 | tf_op jit(solution)/shard_map/all_gather | solution.py:66
  51.9 1.9 slice.96
  53.8 2.2 fusion.32
  56.0 0.6 mul.537
  57.4 1.9 multiply_reduce_fusion.3
  59.3 0.7 multiply_subtract_fusion.10
  60.2 0.8 multiply_subtract_fusion.19
  61.0 0.7 fusion.1
  61.7 0.8 multiply_subtract_fusion.18
  62.5 1.7 multiply_subtract_fusion.9
  64.2 0.7 fusion.3
  64.9 0.8 subtract_bitcast_fusion.3
  65.7 0.8 pad_maximum_fusion.1
  66.6 2.6 %multiply_subtract_fusion.8 = (f32[2048,128]{1,0:T(8,128)S(1)}, f32[2048,128]{1,0:T(8,128)S(1)}) fusion(f32[2048,128]{1,0:T(8,128)S(1)} %get-tuple-element.57, f32[2048,128]{1,0:T(8,128)} %get-tuple-element.58, f32[2048,128]{1,0:T(8,128)} %copy-done.1, f32[2,2048,128]{2,1,0:T(8,128)} %copy-done, bf16[2048,512]{1,0:T(8,128)(2,1)S(1)} %fusion.3, ...), kind=kOutput, calls=%fused_computation.106 | convolution fusion | flops 271646720 | bytes 8650752 | tf_op jit(solution)/shard_map/dot_general | solution.py:34
  69.2 3.8 %collective-permute-done = f32[2,512,128]{2,1,0:T(8,128)} collective-permute-done((f32[2,512,128]{2,1,0:T(8,128)}, f32[2,512,128]{2,1,0:T(8,128)}, u32[]{:S(2)}, u32[]{:S(2)}) %collective-permute-start) | collective-permute-done | bytes 524320 | tf_op jit(solution)/shard_map/ppermute | solution.py:16
  73.0 0.6 mul.573
  73.6 3.7 %multiply_reduce_fusion.2 = (f32[]{:T(128)}, bf16[2048,512]{1,0:T(8,128)(2,1)S(1)}) fusion(f32[256,8,4,128]{3,2,1,0:T(4,128)S(1)} %bitcast.246, bf16[4,2048,512]{2,1,0:T(8,128)(2,1)} %param.7, f32[2,512,128]{2,1,0:T(8,128)} %collective-permute-done, f32[2048,128]{1,0:T(8,128)S(1)} %get-tuple-element.25), kind=kOutput, calls=%fused_computation.36 | convolution fusion | flops 274989056 | bytes 9568260 | tf_op jit(solution)/shard_map/dot_general | solution.py:23
  77.3 1.9 multiply_subtract_fusion.17
  79.3 1.7 multiply_subtract_fusion.7
  81.0 0.7 fusion.5
  81.7 1.7 multiply_subtract_fusion.6
  83.4 1.7 multiply_subtract_fusion.16
  85.1 0.7 fusion.7
  85.9 0.7 multiply_add_fusion.22
  86.6 1.0 subtract_bitcast_fusion.2
  87.7 0.8 pad_maximum_fusion.2
  88.5 4.0 %collective-permute-start.1 = (f32[2,512,128]{2,1,0:T(8,128)}, f32[2,512,128]{2,1,0:T(8,128)}, u32[]{:S(2)}, u32[]{:S(2)}) collective-permute-start(f32[2,512,128]{2,1,0:T(8,128)} %pad_maximum_fusion.2), channel_id=1, source_target_pairs={{0,1},{1,2},{2,3},{3,4},{4,5},{5,6},{6,7},{7,8},{8,9},{9,10},{10,1... | collective-permute-start | bytes 1572872 | tf_op jit(solution)/shard_map/ppermute | solution.py:16
  92.5 1.9 multiply_subtract_fusion.5
  94.5 4.4 %collective-permute-done.1 = f32[2,512,128]{2,1,0:T(8,128)} collective-permute-done((f32[2,512,128]{2,1,0:T(8,128)}, f32[2,512,128]{2,1,0:T(8,128)}, u32[]{:S(2)}, u32[]{:S(2)}) %collective-permute-start.1) | collective-permute-done | bytes 524320 | tf_op jit(solution)/shard_map/ppermute | solution.py:16
  99.5 3.7 %multiply_reduce_fusion.1 = (f32[]{:T(128)}, bf16[2048,512]{1,0:T(8,128)(2,1)S(1)}) fusion(f32[256,8,4,128]{3,2,1,0:T(4,128)S(1)} %bitcast.249, bf16[4,2048,512]{2,1,0:T(8,128)(2,1)} %param.7, f32[2,512,128]{2,1,0:T(8,128)} %collective-permute-done.1, f32[2048,128]{1,0:T(8,128)S(1)} %get-tuple-element.65), kind=kOutput, calls=%fused_computation.35 | convolution fusion | flops 274989056 | bytes 9568260 | tf_op jit(solution)/shard_map/dot_general | solution.py:23
  103.2 1.9 multiply_subtract_fusion.15
  105.2 1.7 multiply_subtract_fusion.4
  106.9 0.7 fusion.9
  107.8 1.8 multiply_subtract_fusion.3
  109.6 1.7 multiply_subtract_fusion.14
  111.3 0.7 fusion.11
  112.0 0.7 multiply_add_fusion.17
  112.8 1.0 subtract_bitcast_fusion.1
  113.8 0.8 pad_maximum_fusion.3
  114.6 4.0 %collective-permute-start.2 = (f32[2,512,128]{2,1,0:T(8,128)}, f32[2,512,128]{2,1,0:T(8,128)}, u32[]{:S(2)}, u32[]{:S(2)}) collective-permute-start(f32[2,512,128]{2,1,0:T(8,128)} %pad_maximum_fusion.3), channel_id=1, source_target_pairs={{0,1},{1,2},{2,3},{3,4},{4,5},{5,6},{6,7},{7,8},{8,9},{9,10},{10,1... | collective-permute-start | bytes 1572872 | tf_op jit(solution)/shard_map/ppermute | solution.py:16
  118.8 2.3 multiply_subtract_fusion.2
  121.1 7.4 %collective-permute-done.2 = f32[2,512,128]{2,1,0:T(8,128)} collective-permute-done((f32[2,512,128]{2,1,0:T(8,128)}, f32[2,512,128]{2,1,0:T(8,128)}, u32[]{:S(2)}, u32[]{:S(2)}) %collective-permute-start.2) | collective-permute-done | bytes 524320 | tf_op jit(solution)/shard_map/ppermute | solution.py:16
  128.5 0.6 mul.645
  129.1 3.7 %multiply_reduce_fusion = (f32[]{:T(128)}, bf16[2048,512]{1,0:T(8,128)(2,1)S(1)}) fusion(f32[256,8,4,128]{3,2,1,0:T(4,128)S(1)} %bitcast.252, bf16[4,2048,512]{2,1,0:T(8,128)(2,1)} %param.7, f32[2,512,128]{2,1,0:T(8,128)} %collective-permute-done.2, f32[2048,128]{1,0:T(8,128)S(1)} %get-tuple-element.19), kind=kOutput, calls=%fused_computation.34 | convolution fusion | flops 274989056 | bytes 9568260 | tf_op jit(solution)/shard_map/dot_general | solution.py:23
  132.8 1.9 multiply_subtract_fusion.13
  134.8 1.8 multiply_subtract_fusion.1
  136.6 0.7 fusion.13
  137.3 0.8 multiply_subtract_fusion
  138.0 2.4 multiply_subtract_fusion.12
  140.5 0.7 fusion.15
  141.2 0.7 subtract_bitcast_fusion
  142.8 2.2 slice.105
  147.6 0.7 maximum_bitcast_fusion
  148.3 0.7 maximum_bitcast_fusion.1
  149.0 0.6 maximum_bitcast_fusion.2
  149.6 0.7 maximum_bitcast_fusion.3
  150.4 93.7 %psum.7 = f32[4,2]{1,0:T(4,128)S(1)} all-reduce(f32[4,2]{1,0:T(4,128)S(1)} %pad_maximum_fusion.4), channel_id=1, replica_groups=mesh['row'=32,'col'=4] {'row','col'}, use_global_device_ids=true, to_apply=%region_11.12 | all-reduce | flops 8 | bytes 64 | tf_op jit(solution)/shard_map/psum | solution.py:88
  244.1 0.7 fusion.115
  244.8 2.6 %multiply_subtract_fusion.11 = (f32[512,128]{1,0:T(8,128)}, f32[512,128]{1,0:T(8,128)}) fusion(f32[512,128]{1,0:T(8,128)S(1)} %get-tuple-element.77, f32[512,128]{1,0:T(8,128)} %get-tuple-element.78, f32[512,128]{1,0:T(8,128)} %copy-done.4, f32[2,512,128]{2,1,0:T(8,128)} %collective-permute-done.2, bf16[2048,512]{1,0:T(8,128)(2,1)S(1)} %fusion.15, ...), kind=kOutput, calls=%fused_computation.127 | convolution fusion | flops 269484032 | bytes 4718592 | tf_op jit(solution)/shard_map/dot_general | solution.py:39
  247.4 2.2 slice_bitcast_fusion.2
  (53 shorter events, 3.2 us)
Async XLA Ops:
  7.2 2.4 copy-start.8
  7.2 4.4 %copy-start.7 = (s32[4,16,4]{1,2,0:T(4,128)S(1)}, s32[4,16,4]{1,2,0:T(4,128)}, u32[]{:S(2)}) copy-start(s32[4,16,4]{1,2,0:T(4,128)} %param.8) | copy-start | bytes 3076
  7.2 44.8 %all-gather.2.cloned.1.call-start = ((), (), s32[]{:S(2)}) async-start(), calls=%async_computation.1 | async-start | bytes 5242880 | tf_op jit(solution)/shard_map/all_gather | solution.py:66
  9.5 237.9 %reduce-scatter.2.cloned.1.call-start = ((), (), s32[]{:S(2)}) async-start(), calls=%async_computation.2 | async-start | bytes 5242880 | tf_op jit(solution)/shard_map/reduce_scatter | solution.py:99
  51.9 4.7 %slice-start = ((s8[8388608]{0:T(1024)(128)(4,1)}), s8[4194304]{0:T(1024)(128)(4,1)S(1)}, s32[]{:S(2)}) async-start(s8[8388608]{0:T(1024)(128)(4,1)} %bitcast.238), calls=%async_computation.3 | async-start | bytes 8388608
  53.8 3.1 %slice-start.1 = ((s8[8388608]{0:T(1024)(128)(4,1)}), s8[4194304]{0:T(1024)(128)(4,1)S(1)}, s32[]{:S(2)}) async-start(s8[8388608]{0:T(1024)(128)(4,1)} %bitcast.238), calls=%async_computation.4 | async-start | bytes 8388608
  56.0 6.5 %copy-start = (f32[2,2048,128]{2,1,0:T(8,128)}, f32[2,2048,128]{2,1,0:T(8,128)S(1)}, u32[]{:S(2)}) copy-start(f32[2,2048,128]{2,1,0:T(8,128)S(1)} %fusion.32) | copy-start | bytes 6291460
  56.0 1.4 copy-start.5
  59.3 0.9 copy-start.6
  60.2 2.3 copy-start.1
  66.5 6.4 %collective-permute-start = (f32[2,512,128]{2,1,0:T(8,128)}, f32[2,512,128]{2,1,0:T(8,128)}, u32[]{:S(2)}, u32[]{:S(2)}) collective-permute-start(f32[2,512,128]{2,1,0:T(8,128)} %pad_maximum_fusion.1), channel_id=1, source_target_pairs={{0,1},{1,2},{2,3},{3,4},{4,5},{5,6},{6,7},{7,8},{8,9},{9,10},{10,1... | collective-permute-start | bytes 1572872 | tf_op jit(solution)/shard_map/ppermute | solution.py:16
  73.6 7.4 %slice-start.2 = ((s8[8388608]{0:T(1024)(128)(4,1)}), s8[4194304]{0:T(1024)(128)(4,1)S(1)}, s32[]{:S(2)}) async-start(s8[8388608]{0:T(1024)(128)(4,1)} %bitcast.240), calls=%async_computation.5 | async-start | bytes 8388608
  77.3 3.6 %slice-start.3 = ((s8[8388608]{0:T(1024)(128)(4,1)}), s8[4194304]{0:T(1024)(128)(4,1)S(1)}, s32[]{:S(2)}) async-start(s8[8388608]{0:T(1024)(128)(4,1)} %bitcast.240), calls=%async_computation.6 | async-start | bytes 8388608
  88.5 10.4 %collective-permute-start.1 = (f32[2,512,128]{2,1,0:T(8,128)}, f32[2,512,128]{2,1,0:T(8,128)}, u32[]{:S(2)}, u32[]{:S(2)}) collective-permute-start(f32[2,512,128]{2,1,0:T(8,128)} %pad_maximum_fusion.2), channel_id=1, source_target_pairs={{0,1},{1,2},{2,3},{3,4},{4,5},{5,6},{6,7},{7,8},{8,9},{9,10},{10,1... | collective-permute-start | bytes 1572872 | tf_op jit(solution)/shard_map/ppermute | solution.py:16
  99.5 7.4 %slice-start.4 = ((s8[8388608]{0:T(1024)(128)(4,1)}), s8[4194304]{0:T(1024)(128)(4,1)S(1)}, s32[]{:S(2)}) async-start(s8[8388608]{0:T(1024)(128)(4,1)} %bitcast.242), calls=%async_computation.7 | async-start | bytes 8388608
  103.2 1.9 copy-start.2
  103.2 3.7 %slice-start.5 = ((s8[8388608]{0:T(1024)(128)(4,1)}), s8[4194304]{0:T(1024)(128)(4,1)S(1)}, s32[]{:S(2)}) async-start(s8[8388608]{0:T(1024)(128)(4,1)} %bitcast.242), calls=%async_computation.8 | async-start | bytes 8388608
  106.9 0.9 copy-start.3
  114.6 13.9 %collective-permute-start.2 = (f32[2,512,128]{2,1,0:T(8,128)}, f32[2,512,128]{2,1,0:T(8,128)}, u32[]{:S(2)}, u32[]{:S(2)}) collective-permute-start(f32[2,512,128]{2,1,0:T(8,128)} %pad_maximum_fusion.3), channel_id=1, source_target_pairs={{0,1},{1,2},{2,3},{3,4},{4,5},{5,6},{6,7},{7,8},{8,9},{9,10},{10,1... | collective-permute-start | bytes 1572872 | tf_op jit(solution)/shard_map/ppermute | solution.py:16
  129.1 7.4 %slice-start.6 = ((s8[8388608]{0:T(1024)(128)(4,1)}), s8[4194304]{0:T(1024)(128)(4,1)S(1)}, s32[]{:S(2)}) async-start(s8[8388608]{0:T(1024)(128)(4,1)} %bitcast.244), calls=%async_computation.9 | async-start | bytes 8388608
  132.8 3.7 %slice-start.7 = ((s8[8388608]{0:T(1024)(128)(4,1)}), s8[4194304]{0:T(1024)(128)(4,1)S(1)}, s32[]{:S(2)}) async-start(s8[8388608]{0:T(1024)(128)(4,1)} %bitcast.244), calls=%async_computation.10 | async-start | bytes 8388608
  134.7 3.3 %copy-start.4 = (f32[512,128]{1,0:T(8,128)}, f32[512,128]{1,0:T(8,128)S(1)}, u32[]{:S(2)}) copy-start(f32[512,128]{1,0:T(8,128)S(1)} %get-tuple-element.76) | copy-start | bytes 786436
Sparse Core Ops, SparseCore 0:
  9.7 42.2 all-gather.1
  145.1 56.8 reduce-scatter.1
where the time goes:
time: 257 us
  blocking collectives  93.7 us (36%)
  matrix products  56 us (22%)
  waiting for transfers between devices  55.2 us (21%)
  between operations  17.7 us (7%)
  other arithmetic  15 us (6%)
  local copies, waits for them, and re-layouts  10.8 us (4%)
  starting transfers between devices  8.05 us (3%)
    psum x1, blocking collectives, on_device(): loss_parts = lax.psum(jnp.stack(loss_list), ('row', 'col'))  93.7 us
    all_gather x1, waiting for transfers between devices, on_device(): lax.all_gather(jnp.stack([users, user_accum]), 'col', axis=1, tiled=True)  39.6 us
    dot_general x12, matrix products, update(): jnp.dot(err_half, item_half, preferred_element_type=jnp.float32)  19.3 us
    dot_general x12, matrix products, update(): lax.dot_general(user_half, item_half, (((1,), (1,)), ((), ())), preferred...  18.7 us
    dot_general x12, matrix products, update(): lax.dot_general(err_half, user_half, (((0,), (0,)), ((), ())), preferred_...  18.1 us
    ppermute x3, waiting for transfers between devices, passed_along(): return lax.ppermute(value, axis, pairs)  15.6 us
    ppermute x3, starting transfers between devices, passed_along(): return lax.ppermute(value, axis, pairs)  7.97 us
  transfers between devices with their start and end apart: 5, of which 4 were waited for; matrix products, arithmetic and copies ran while one was open for 6% of the time, Pallas kernels for 0%

commit v1 on v0

--- a/solution.py
+++ b/solution.py
@@ -63,7 +63,12 @@
     start_tile = jnp.sum(jnp.where(ranks < member, group_counts, 0))
     own_count = jnp.sum(jnp.where(ranks == member, group_counts, 0))
     valid = (jnp.arange(slot_count, dtype=jnp.int32) < own_count).astype(jnp.float32)
-    whole_pair = lax.all_gather(jnp.stack([users, user_accum]), "col", axis=1, tiled=True)
+    whole_pair = jnp.concatenate(
+        lax.all_to_all(
+            jnp.stack([jnp.stack([users, user_accum])] * lax.axis_size("col")), "col", 0, 0
+        ),
+        axis=1,
+    )
     pad_rows = slot_count * tile_size
     ext_pair = jnp.concatenate([whole_pair, whole_pair[:, :pad_rows]], axis=1)
     user_pair = lax.dynamic_slice_in_dim(ext_pair, start_tile * tile_size, pad_rows, 1)

time: 257 us -> 276 us (1.074)
  starting transfers between devices: 8.05 us -> 15.7 us
  waiting for transfers between devices: 55.2 us -> 61.3 us
  local copies, waits for them, and re-layouts: 10.8 us -> 15.9 us
    all_to_all x0 -> x1, waiting for transfers between devices: none -> 45.9 us  [on_device(): lax.all_to_all(jnp.stack([jnp.stack([users, user_accum])] * lax.axis_size...]
    all_gather x1 -> x0, waiting for transfers between devices: 39.6 us -> none  [on_device(): lax.all_gather(jnp.stack([users, user_accum]), 'col', axis=1, tiled=True)]
    all_to_all x0 -> x1, starting transfers between devices: none -> 6.77 us  [on_device(): lax.all_to_all(jnp.stack([jnp.stack([users, user_accum])] * lax.axis_size...]
where the time goes in v1:
time: 276 us; the launch traced here: 275 us
  blocking collectives  96 us (35%)
  waiting for transfers between devices  61.3 us (22%)
  matrix products  56.1 us (20%)
  between operations  17.8 us (6%)
  local copies, waits for them, and re-layouts  15.9 us (6%)
  starting transfers between devices  15.7 us (6%)
  other arithmetic  12.6 us (5%)
    psum x1, blocking collectives, on_device(): loss_parts = lax.psum(jnp.stack(loss_list), ('row', 'col'))  96 us
    all_to_all x1, waiting for transfers between devices, on_device(): lax.all_to_all(jnp.stack([jnp.stack([users, user_accum])] * lax.axis_size...  45.9 us
    dot_general x12, matrix products, update(): jnp.dot(err_half, item_half, preferred_element_type=jnp.float32)  19.3 us
    dot_general x12, matrix products, update(): lax.dot_general(user_half, item_half, (((1,), (1,)), ((), ())), preferred...  18.7 us
    dot_general x12, matrix products, update(): lax.dot_general(err_half, user_half, (((0,), (0,)), ((), ())), preferred_...  18.1 us
    ppermute x3, waiting for transfers between devices, passed_along(): return lax.ppermute(value, axis, pairs)  15.4 us
    ppermute x3, starting transfers between devices, passed_along(): return lax.ppermute(value, axis, pairs)  8.96 us
    all_to_all x1, starting transfers between devices, on_device(): lax.all_to_all(jnp.stack([jnp.stack([users, user_accum])] * lax.axis_size...  6.77 us
  transfers between devices with their start and end apart: 5, of which 4 were waited for; matrix products, arithmetic and copies ran while one was open for 6% of the time, Pallas kernels for 0%

profile of v1, /device:TPU:1, one launch (start us, length us, event | category | flops | bytes accessed | tf_op | source)
XLA Modules:
  0.0 275.4 jit_solution(10104780398952972332)
XLA Ops:
  7.2 1.3 pad_maximum_fusion
  8.4 2.3 stack.106
  10.7 6.8 %all-to-all-start = ((f32[4,2,1024,128]{3,2,1,0:T(8,128)}), f32[4,2,1024,128]{3,2,1,0:T(8,128)}, u32[]{:S(2)}, u32[]{:S(2)}) async-start(f32[4,2,1024,128]{3,2,1,0:T(8,128)} %stack.106), calls=%async_computation | async-start | bytes 8388608 | tf_op jit(solution)/shard_map/all_to_all | solution.py:67
  17.5 0.7 fusion.116
  19.5 0.7 fusion.121
  20.3 45.9 %all-to-all-done = f32[4,2,1024,128]{3,2,1,0:T(8,128)} async-done(((f32[4,2,1024,128]{3,2,1,0:T(8,128)}), f32[4,2,1024,128]{3,2,1,0:T(8,128)}, u32[]{:S(2)}, u32[]{:S(2)}) %all-to-all-start) | async-done | bytes 4194336 | tf_op jit(solution)/shard_map/all_to_all | solution.py:67
  66.3 2.5 copy.20
  70.2 1.5 slice-done
  71.7 1.3 slice-done.1
  73.0 1.9 multiply_reduce_fusion.3
  74.9 0.7 multiply_subtract_fusion.10
  75.9 0.8 multiply_subtract_fusion.19
  76.6 0.7 fusion.1
  77.4 0.8 multiply_subtract_fusion.18
  78.2 1.7 multiply_subtract_fusion.9
  79.9 0.7 fusion.3
  80.6 0.8 subtract_bitcast_fusion.3
  81.3 0.8 pad_maximum_fusion.1
  82.2 1.0 collective-permute-start
  83.3 2.6 multiply_subtract_fusion.8
  85.8 3.8 %collective-permute-done = f32[2,512,128]{2,1,0:T(8,128)} collective-permute-done((f32[2,512,128]{2,1,0:T(8,128)}, f32[2,512,128]{2,1,0:T(8,128)}, u32[]{:S(2)}, u32[]{:S(2)}) %collective-permute-start) | collective-permute-done | bytes 524320 | tf_op jit(solution)/shard_map/ppermute | solution.py:16
  90.2 3.7 %multiply_reduce_fusion.2 = (f32[]{:T(128)}, bf16[2048,512]{1,0:T(8,128)(2,1)S(1)}) fusion(f32[256,8,4,128]{3,2,1,0:T(4,128)S(1)} %bitcast.248, bf16[4,2048,512]{2,1,0:T(8,128)(2,1)} %param.7, f32[2,512,128]{2,1,0:T(8,128)} %collective-permute-done, f32[2048,128]{1,0:T(8,128)S(1)} %get-tuple-element.25), kind=kOutput, calls=%fused_computation.36 | convolution fusion | flops 274989056 | bytes 9568260 | tf_op jit(solution)/shard_map/dot_general | solution.py:23
  93.9 1.9 multiply_subtract_fusion.17
  95.9 1.7 multiply_subtract_fusion.7
  97.6 0.7 fusion.5
  98.3 1.7 multiply_subtract_fusion.6
  100.0 1.7 multiply_subtract_fusion.16
  101.8 0.7 fusion.7
  102.5 0.7 multiply_add_fusion.22
  103.2 1.0 subtract_bitcast_fusion.2
  104.3 0.8 pad_maximum_fusion.2
  105.1 4.0 %collective-permute-start.1 = (f32[2,512,128]{2,1,0:T(8,128)}, f32[2,512,128]{2,1,0:T(8,128)}, u32[]{:S(2)}, u32[]{:S(2)}) collective-permute-start(f32[2,512,128]{2,1,0:T(8,128)} %pad_maximum_fusion.2), channel_id=1, source_target_pairs={{0,1},{1,2},{2,3},{3,4},{4,5},{5,6},{6,7},{7,8},{8,9},{9,10},{10,1... | collective-permute-start | bytes 1572872 | tf_op jit(solution)/shard_map/ppermute | solution.py:16
  109.2 1.9 multiply_subtract_fusion.5
  111.1 4.4 %collective-permute-done.1 = f32[2,512,128]{2,1,0:T(8,128)} collective-permute-done((f32[2,512,128]{2,1,0:T(8,128)}, f32[2,512,128]{2,1,0:T(8,128)}, u32[]{:S(2)}, u32[]{:S(2)}) %collective-permute-start.1) | collective-permute-done | bytes 524320 | tf_op jit(solution)/shard_map/ppermute | solution.py:16
  116.2 3.7 %multiply_reduce_fusion.1 = (f32[]{:T(128)}, bf16[2048,512]{1,0:T(8,128)(2,1)S(1)}) fusion(f32[256,8,4,128]{3,2,1,0:T(4,128)S(1)} %bitcast.251, bf16[4,2048,512]{2,1,0:T(8,128)(2,1)} %param.7, f32[2,512,128]{2,1,0:T(8,128)} %collective-permute-done.1, f32[2048,128]{1,0:T(8,128)S(1)} %get-tuple-element.65), kind=kOutput, calls=%fused_computation.35 | convolution fusion | flops 274989056 | bytes 9568260 | tf_op jit(solution)/shard_map/dot_general | solution.py:23
  119.9 1.9 multiply_subtract_fusion.15
  121.9 1.7 multiply_subtract_fusion.4
  123.6 0.7 fusion.9
  124.5 1.8 multiply_subtract_fusion.3
  126.3 1.7 multiply_subtract_fusion.14
  128.0 0.7 fusion.11
  128.7 0.7 multiply_add_fusion.17
  129.5 1.0 subtract_bitcast_fusion.1
  130.5 0.8 pad_maximum_fusion.3
  131.4 4.0 %collective-permute-start.2 = (f32[2,512,128]{2,1,0:T(8,128)}, f32[2,512,128]{2,1,0:T(8,128)}, u32[]{:S(2)}, u32[]{:S(2)}) collective-permute-start(f32[2,512,128]{2,1,0:T(8,128)} %pad_maximum_fusion.3), channel_id=1, source_target_pairs={{0,1},{1,2},{2,3},{3,4},{4,5},{5,6},{6,7},{7,8},{8,9},{9,10},{10,1... | collective-permute-start | bytes 1572872 | tf_op jit(solution)/shard_map/ppermute | solution.py:16
  135.5 2.3 multiply_subtract_fusion.2
  137.8 7.2 %collective-permute-done.2 = f32[2,512,128]{2,1,0:T(8,128)} collective-permute-done((f32[2,512,128]{2,1,0:T(8,128)}, f32[2,512,128]{2,1,0:T(8,128)}, u32[]{:S(2)}, u32[]{:S(2)}) %collective-permute-start.2) | collective-permute-done | bytes 524320 | tf_op jit(solution)/shard_map/ppermute | solution.py:16
  145.6 3.7 %multiply_reduce_fusion = (f32[]{:T(128)}, bf16[2048,512]{1,0:T(8,128)(2,1)S(1)}) fusion(f32[256,8,4,128]{3,2,1,0:T(4,128)S(1)} %bitcast.254, bf16[4,2048,512]{2,1,0:T(8,128)(2,1)} %param.7, f32[2,512,128]{2,1,0:T(8,128)} %collective-permute-done.2, f32[2048,128]{1,0:T(8,128)S(1)} %get-tuple-element.19), kind=kOutput, calls=%fused_computation.34 | convolution fusion | flops 274989056 | bytes 9568260 | tf_op jit(solution)/shard_map/dot_general | solution.py:23
  149.2 1.9 multiply_subtract_fusion.13
  151.2 1.8 multiply_subtract_fusion.1
  153.0 0.7 fusion.13
  153.7 0.8 multiply_subtract_fusion
  154.5 2.4 multiply_subtract_fusion.12
  156.9 0.7 fusion.15
  157.6 0.7 subtract_bitcast_fusion
  159.2 2.2 slice.105
  164.1 0.7 maximum_bitcast_fusion
  164.8 0.7 maximum_bitcast_fusion.1
  165.5 0.7 maximum_bitcast_fusion.2
  166.2 0.7 maximum_bitcast_fusion.3
  167.0 96.0 %psum.7 = f32[4,2]{1,0:T(4,128)S(1)} all-reduce(f32[4,2]{1,0:T(4,128)S(1)} %pad_maximum_fusion.4), channel_id=1, replica_groups=mesh['row'=32,'col'=4] {'row','col'}, use_global_device_ids=true, to_apply=%region_11.12 | all-reduce | flops 8 | bytes 64 | tf_op jit(solution)/shard_map/psum | solution.py:93
  263.0 0.7 fusion.115
  263.7 2.6 multiply_subtract_fusion.11
  266.3 2.2 slice_bitcast_fusion.2
  (54 shorter events, 5.6 us)
Async XLA Ops:
  10.7 6.8 %copy-start.8 = (s32[128]{0:T(128)S(1)}, s32[128]{0:T(128)}, u32[]{:S(2)}) copy-start(s32[128]{0:T(128)} %param.9) | copy-start | bytes 1540
  10.7 8.8 %copy-start.7 = (s32[4,16,4]{1,2,0:T(4,128)S(1)}, s32[4,16,4]{1,2,0:T(4,128)}, u32[]{:S(2)}) copy-start(s32[4,16,4]{1,2,0:T(4,128)} %param.8) | copy-start | bytes 3076
  10.7 55.5 %all-to-all-start = ((f32[4,2,1024,128]{3,2,1,0:T(8,128)}), f32[4,2,1024,128]{3,2,1,0:T(8,128)}, u32[]{:S(2)}, u32[]{:S(2)}) async-start(f32[4,2,1024,128]{3,2,1,0:T(8,128)} %stack.106), calls=%async_computation | async-start | bytes 8388608 | tf_op jit(solution)/shard_map/all_to_all | solution.py:67
  17.5 248.8 %reduce-scatter.2.cloned.1.call-start = ((), (), s32[]{:S(2)}) async-start(), calls=%async_computation.2 | async-start | bytes 5242880 | tf_op jit(solution)/shard_map/reduce_scatter | solution.py:104
  68.7 2.9 %slice-start = ((s8[8388608]{0:T(1024)(128)(4,1)}), s8[4194304]{0:T(1024)(128)(4,1)S(1)}, s32[]{:S(2)}) async-start(s8[8388608]{0:T(1024)(128)(4,1)} %bitcast.240), calls=%async_computation.3 | async-start | bytes 8388608
  68.9 4.1 %slice-start.1 = ((s8[8388608]{0:T(1024)(128)(4,1)}), s8[4194304]{0:T(1024)(128)(4,1)S(1)}, s32[]{:S(2)}) async-start(s8[8388608]{0:T(1024)(128)(4,1)} %bitcast.240), calls=%async_computation.4 | async-start | bytes 8388608
  69.5 8.6 %copy-start = (f32[2,2048,128]{2,1,0:T(8,128)}, f32[2,2048,128]{2,1,0:T(8,128)S(1)}, u32[]{:S(2)}) copy-start(f32[2,2048,128]{2,1,0:T(8,128)S(1)} %fusion.32) | copy-start | bytes 6291460
  69.6 3.5 %copy-start.5 = (f32[512,128]{1,0:T(8,128)S(1)}, f32[512,128]{1,0:T(8,128)}, u32[]{:S(2)}) copy-start(f32[512,128]{1,0:T(8,128)} %param.12) | copy-start | bytes 786436
  74.9 0.9 copy-start.6
  75.9 2.3 copy-start.1
  82.2 7.4 %collective-permute-start = (f32[2,512,128]{2,1,0:T(8,128)}, f32[2,512,128]{2,1,0:T(8,128)}, u32[]{:S(2)}, u32[]{:S(2)}) collective-permute-start(f32[2,512,128]{2,1,0:T(8,128)} %pad_maximum_fusion.1), channel_id=1, source_target_pairs={{0,1},{1,2},{2,3},{3,4},{4,5},{5,6},{6,7},{7,8},{8,9},{9,10},{10,1... | collective-permute-start | bytes 1572872 | tf_op jit(solution)/shard_map/ppermute | solution.py:16
  90.2 7.3 %slice-start.2 = ((s8[8388608]{0:T(1024)(128)(4,1)}), s8[4194304]{0:T(1024)(128)(4,1)S(1)}, s32[]{:S(2)}) async-start(s8[8388608]{0:T(1024)(128)(4,1)} %bitcast.242), calls=%async_computation.5 | async-start | bytes 8388608
  93.9 3.6 %slice-start.3 = ((s8[8388608]{0:T(1024)(128)(4,1)}), s8[4194304]{0:T(1024)(128)(4,1)S(1)}, s32[]{:S(2)}) async-start(s8[8388608]{0:T(1024)(128)(4,1)} %bitcast.242), calls=%async_computation.6 | async-start | bytes 8388608
  105.1 10.4 %collective-permute-start.1 = (f32[2,512,128]{2,1,0:T(8,128)}, f32[2,512,128]{2,1,0:T(8,128)}, u32[]{:S(2)}, u32[]{:S(2)}) collective-permute-start(f32[2,512,128]{2,1,0:T(8,128)} %pad_maximum_fusion.2), channel_id=1, source_target_pairs={{0,1},{1,2},{2,3},{3,4},{4,5},{5,6},{6,7},{7,8},{8,9},{9,10},{10,1... | collective-permute-start | bytes 1572872 | tf_op jit(solution)/shard_map/ppermute | solution.py:16
  116.1 7.4 %slice-start.4 = ((s8[8388608]{0:T(1024)(128)(4,1)}), s8[4194304]{0:T(1024)(128)(4,1)S(1)}, s32[]{:S(2)}) async-start(s8[8388608]{0:T(1024)(128)(4,1)} %bitcast.244), calls=%async_computation.7 | async-start | bytes 8388608
  119.9 1.9 copy-start.2
  119.9 3.7 %slice-start.5 = ((s8[8388608]{0:T(1024)(128)(4,1)}), s8[4194304]{0:T(1024)(128)(4,1)S(1)}, s32[]{:S(2)}) async-start(s8[8388608]{0:T(1024)(128)(4,1)} %bitcast.244), calls=%async_computation.8 | async-start | bytes 8388608
  123.5 1.0 copy-start.3
  131.4 13.6 %collective-permute-start.2 = (f32[2,512,128]{2,1,0:T(8,128)}, f32[2,512,128]{2,1,0:T(8,128)}, u32[]{:S(2)}, u32[]{:S(2)}) collective-permute-start(f32[2,512,128]{2,1,0:T(8,128)} %pad_maximum_fusion.3), channel_id=1, source_target_pairs={{0,1},{1,2},{2,3},{3,4},{4,5},{5,6},{6,7},{7,8},{8,9},{9,10},{10,1... | collective-permute-start | bytes 1572872 | tf_op jit(solution)/shard_map/ppermute | solution.py:16
  145.6 7.4 %slice-start.6 = ((s8[8388608]{0:T(1024)(128)(4,1)}), s8[4194304]{0:T(1024)(128)(4,1)S(1)}, s32[]{:S(2)}) async-start(s8[8388608]{0:T(1024)(128)(4,1)} %bitcast.246), calls=%async_computation.9 | async-start | bytes 8388608
  149.2 3.7 %slice-start.7 = ((s8[8388608]{0:T(1024)(128)(4,1)}), s8[4194304]{0:T(1024)(128)(4,1)S(1)}, s32[]{:S(2)}) async-start(s8[8388608]{0:T(1024)(128)(4,1)} %bitcast.246), calls=%async_computation.10 | async-start | bytes 8388608
  151.2 3.3 %copy-start.4 = (f32[512,128]{1,0:T(8,128)}, f32[512,128]{1,0:T(8,128)S(1)}, u32[]{:S(2)}) copy-start(f32[512,128]{1,0:T(8,128)S(1)} %get-tuple-element.76) | copy-start | bytes 786436
Sparse Core Ops, SparseCore 0:
  161.6 56.8 reduce-scatter.1
